TPU v7x, 32 devices: a whole 2x2x4 slice. The times are simulated.
32 devices in a mesh: seq: 8 (over y, x, core), head: 4 (over z).
Axes of the slice: x: 2, y: 2, z: 4, core: 2. Of those that a mesh axis runs over, the one named last changes fastest.
Arguments:
- tokens: bfloat16 [4096, 5376], P('seq', 'head'), may hold values from -32 to 32
- query_weight: bfloat16 [5376, 4096], P(None, 'head'), may hold values from -1 to 1
- key_weight: bfloat16 [5376, 2048], P(None, 'head'), may hold values from -1 to 1
- value_weight: bfloat16 [5376, 2048], P(None, 'head'), may hold values from -0.078125 to 0.078125
- output_grad: bfloat16 [4096, 4096], P('seq', 'head'), may hold values from -48 to 48
- segments: int32 [4096], replicated, may hold values from 0 to 3, never falling along the last dimension, each value on 1 to 2048 neighbouring positions
Outputs:
- token_grad: bfloat16 [4096, 5376], P('seq', 'head')
- query_weight_grad: bfloat16 [5376, 4096], P('seq', 'head')
- key_weight_grad: bfloat16 [5376, 2048], P('seq', 'head')
- value_weight_grad: bfloat16 [5376, 2048], P('seq', 'head')
Inputs may be any that keep to these rules, and one draw needn't show every extreme that they name: `segments`: segment numbers never fall along the tokens; a segment has at most 2048 tokens.
All inputs are finite; a program needn't handle non-finite values.
Results may differ from a plain program's by a relative error of at most 0.015.
The roundings to bfloat16 on the way count: a program that leaves them out, or rounds other values in their place, can miss the bound.
Values may be sent and summed in bfloat16 or wider, within the bound.
No kernel may reach another device: no remote copies, remote signals or barrier semaphores. Data moves between devices by JAX's collectives and lax.ppermute only.
A program may use at most 192 MiB of HBM per device.

v0:
```python
import jax
import jax.numpy as jnp
from jax import lax
from jax.sharding import Mesh, PartitionSpec as P

D = 5376
HEADS = 32
KV_HEADS = 16
HEAD_DIM = 128
WINDOW = 1024
HOPS = 2
SEQ = ("seq_hi", "core")
neg_large = -1e30


def passed_along(x, axis, by):
    count = lax.axis_size(axis)
    pairs = [(i, i + by) for i in range(count) if 0 <= i + by < count]
    return lax.ppermute(x, axis, pairs)


def contract_last(left, right):
    return lax.dot_general(
        left, right, (((1,), (1,)), ((), ())), preferred_element_type=jnp.float32
    )


def contract_first(left, right):
    return lax.dot_general(
        left, right, (((0,), (0,)), ((), ())), preferred_element_type=jnp.float32
    )


def attend(queries, key_value, grads, query_first, key_first, seg_query, seg_key):
    tok_rows = queries.shape[0]
    key_rows = key_value.shape[1]
    groups = HEADS // KV_HEADS
    kv_local = key_value.shape[2] // HEAD_DIM
    score_scale = (D / HEADS) ** (-0.5)
    query_four = queries.reshape(tok_rows, kv_local, groups, HEAD_DIM)
    grad_four = grads.reshape(tok_rows, kv_local, groups, HEAD_DIM)
    key_three = key_value[0].reshape(key_rows, kv_local, HEAD_DIM)
    value_three = key_value[1].reshape(key_rows, kv_local, HEAD_DIM)
    query_pos = query_first + jnp.arange(tok_rows, dtype=jnp.int32)
    key_pos = key_first + jnp.arange(key_rows, dtype=jnp.int32)
    spacing = query_pos[:, None] - key_pos[None, :]
    allowed = (
        (key_pos >= 0)[None, :]
        & (spacing >= 0)
        & (spacing < WINDOW)
        & (seg_query[:, None] == seg_key[None, :])
    )
    scores = (
        jnp.einsum("akgd,ckd->kgac", query_four, key_three, preferred_element_type=jnp.float32)
        * score_scale
    )
    masked = jnp.where(allowed, scores, neg_large)
    row_max = jnp.max(masked, axis=-1, keepdims=True)
    expo = jnp.where(allowed, jnp.exp(masked - row_max), 0.0)
    probs = expo / jnp.sum(expo, axis=-1, keepdims=True)
    dprobs = jnp.einsum(
        "akgd,ckd->kgac", grad_four, value_three, preferred_element_type=jnp.float32
    )
    center = jnp.sum(probs * dprobs, axis=-1, keepdims=True)
    dscores = (probs * (dprobs - center)).astype(jnp.bfloat16)
    probs_low = probs.astype(jnp.bfloat16)
    query_grad = (
        (
            jnp.einsum("kgac,ckd->akgd", dscores, key_three, preferred_element_type=jnp.float32)
            * score_scale
        )
        .reshape(tok_rows, -1)
        .astype(jnp.bfloat16)
    )
    key_grad = (
        jnp.einsum("kgac,akgd->ckd", dscores, query_four, preferred_element_type=jnp.float32)
        * score_scale
    ).reshape(key_rows, -1)
    value_grad = jnp.einsum(
        "kgac,akgd->ckd", probs_low, grad_four, preferred_element_type=jnp.float32
    ).reshape(key_rows, -1)
    return (query_grad, jnp.stack([key_grad, value_grad]))


def per_device(tokens, query_weight, key_weight, value_weight, output_grad, segments):
    tok_rows = tokens.shape[0]
    hop_count = HOPS
    margin = hop_count * tok_rows
    gathered = lax.all_gather(tokens, "head", axis=1, tiled=True)
    queries = jnp.dot(gathered, query_weight, preferred_element_type=jnp.float32).astype(
        jnp.bfloat16
    )
    keys_own = jnp.dot(gathered, key_weight, preferred_element_type=jnp.float32).astype(
        jnp.bfloat16
    )
    values_own = jnp.dot(gathered, value_weight, preferred_element_type=jnp.float32).astype(
        jnp.bfloat16
    )
    key_value = jnp.stack([keys_own, values_own])
    blocks = [key_value] * (hop_count + 1)
    for distance in range(1, hop_count + 1):
        blocks[hop_count - distance] = passed_along(key_value, SEQ, distance)
    keys_all = jnp.concatenate(blocks, axis=1)
    position = lax.axis_index(SEQ)
    query_first = position * tok_rows
    seg_query = lax.dynamic_slice_in_dim(segments, query_first, tok_rows, 0)
    seg_padded = jnp.concatenate([jnp.full((margin,), -1, jnp.int32), segments], axis=0)
    seg_key = lax.dynamic_slice_in_dim(seg_padded, query_first, (hop_count + 1) * tok_rows, 0)
    query_grad, kv_grad = attend(
        queries, keys_all, output_grad, query_first, query_first - margin, seg_query, seg_key
    )
    pieces = [
        kv_grad[:, block * tok_rows : (block + 1) * tok_rows] for block in range(hop_count + 1)
    ]
    carried = pieces[hop_count]
    for distance in range(1, hop_count + 1):
        back = passed_along(pieces[hop_count - distance].astype(jnp.bfloat16), SEQ, -distance)
        carried = carried + back.astype(jnp.float32)
    key_grad = carried[0].astype(jnp.bfloat16)
    value_grad = carried[1].astype(jnp.bfloat16)
    n_head = lax.axis_size("head")
    me = lax.axis_index("head")
    width = tokens.shape[1]

    def term(dest):
        start = dest * width
        part = contract_last(query_grad, lax.dynamic_slice_in_dim(query_weight, start, width, 0))
        part = part + contract_last(key_grad, lax.dynamic_slice_in_dim(key_weight, start, width, 0))
        part = part + contract_last(
            value_grad, lax.dynamic_slice_in_dim(value_weight, start, width, 0)
        )
        return part.astype(jnp.bfloat16)

    token_sum = None
    for shift in range(n_head - 1, 0, -1):
        sent = term((me + shift) % n_head)
        pairs = [(i, (i + shift) % n_head) for i in range(n_head)]
        got = lax.ppermute(sent, "head", pairs).astype(jnp.float32)
        token_sum = got if token_sum is None else token_sum + got
    own = term(me).astype(jnp.float32)
    token_grad = (own if token_sum is None else token_sum + own).astype(jnp.bfloat16)
    proj_grads = jnp.concatenate([query_grad, key_grad, value_grad], axis=1)
    weight_part = contract_first(proj_grads, gathered).astype(jnp.bfloat16)
    n_seq = lax.axis_size(SEQ)
    block = weight_part.shape[1] // n_seq

    def weight_block(dest):
        return lax.dynamic_slice_in_dim(weight_part, dest * block, block, 1)

    weight_sum = weight_block(position).astype(jnp.float32)
    for shift in range(n_seq - 1, 0, -1):
        sent = weight_block((position + shift) % n_seq)
        pairs = [(i, (i + shift) % n_seq) for i in range(n_seq)]
        weight_sum = weight_sum + lax.ppermute(sent, SEQ, pairs).astype(jnp.float32)
    summed = (weight_sum * (tok_rows * n_seq) ** (-0.5)).astype(jnp.bfloat16).T
    q_width = query_weight.shape[1]
    k_width = key_weight.shape[1]
    query_weight_grad = summed[:, :q_width]
    key_weight_grad = summed[:, q_width : q_width + k_width]
    value_weight_grad = summed[:, q_width + k_width :]
    return (token_grad, query_weight_grad, key_weight_grad, value_weight_grad)


def solution(mesh):
    n_seq = mesh.shape["seq"]
    n_head = mesh.shape["head"]
    view = Mesh(mesh.devices.reshape(n_seq // 2, 2, n_head), ("seq_hi", "core", "head"))
    in_specs = (
        P(SEQ, "head"),
        P(None, "head"),
        P(None, "head"),
        P(None, "head"),
        P(SEQ, "head"),
        P(),
    )
    out_specs = (P(SEQ, "head"),) * 4
    return jax.shard_map(
        per_device, mesh=view, in_specs=in_specs, out_specs=out_specs, check_vma=False
    )
```

profile of v0, /device:TPU:27, one launch (start us, length us, event | category | flops | bytes accessed | tf_op | source)
XLA Modules:
  0.0 638.8 jit_solution(9430814455776416603)
XLA Ops:
  7.2 0.7 all-gather.2.cloned.1.call-update
  8.0 2.3 copy.77
  10.3 0.1 dynamic_slice.66
  10.4 0.1 pad_dynamic-slice_fusion
  10.5 2.6 fusion.16
  13.1 97.3 %all-gather.2.cloned.1.call-done = bf16[512,5376]{0,1:T(8,128)(2,1)} async-done(((bf16[512,1344]{0,1:T(8,128)(2,1)}), bf16[512,5376]{0,1:T(8,128)(2,1)}) %all-gather.2.cloned.1.call-update) | async-done | bytes 5505040 | tf_op jit(solution)/shard_map/all_gather | solution.py:89
  110.5 7.3 %fusion.53 = bf16[1,512,512]{2,1,0:T(8,128)(2,1)S(1)} fusion(bf16[512,5376]{0,1:T(8,128)(2,1)} %all-gather.2.cloned.1.call-done, bf16[5376,512]{1,0:T(8,128)(2,1)} %param.9), kind=kOutput, calls=%fused_computation.77 | convolution fusion | flops 2818834432 | bytes 11534336 | tf_op jit(solution)/shard_map/dot_general | solution.py:96
  117.9 5.7 fusion.52
  123.6 0.1 pad_maximum_fusion.1
  123.7 3.4 collective-permute-start.1
  127.2 3.1 collective-permute-start
  130.3 5.9 convolution_convert_fusion.1
  136.2 1.9 copy.76
  138.1 9.5 %collective-permute-done.1 = bf16[2,512,512]{2,1,0:T(8,128)(2,1)} collective-permute-done((bf16[2,512,512]{2,1,0:T(8,128)(2,1)S(1)}, bf16[2,512,512]{2,1,0:T(8,128)(2,1)}, u32[]{:S(2)}, u32[]{:S(2)}) %collective-permute-start.1) | collective-permute-done | bytes 1048608 | tf_op jit(solution)/shard_map/ppermute | solution.py:19
  147.5 14.7 %collective-permute-done = bf16[2,512,512]{2,1,0:T(8,128)(2,1)} collective-permute-done((bf16[2,512,512]{2,1,0:T(8,128)(2,1)S(1)}, bf16[2,512,512]{2,1,0:T(8,128)(2,1)}, u32[]{:S(2)}, u32[]{:S(2)}) %collective-permute-start) | collective-permute-done | bytes 1048608 | tf_op jit(solution)/shard_map/ppermute | solution.py:19
  162.2 1.7 maximum_maximum_fusion
  163.9 1.4 fusion.70
  165.3 0.4 reshape_squeeze.6
  165.7 1.0 copy.63
  166.7 4.0 reshape_squeeze.7
  170.8 13.6 %fusion.72 = (f32[4,2,512]{2,1,0:T(2,128)S(1)}, f32[4,2,512,1536]{2,3,1,0:T(8,128)}) fusion(pred[512,1536]{0,1:T(8,128)(4,1)S(1)} %copy-done.11, bf16[1536,4,128,1]{0,2,3,1:T(8,128)(2,1)S(1)} %copy.63, bf16[512,4,2,128]{0,3,2,1:T(8,128)(2,1)S(1)} %bitcast.81), kind=kOutput, calls=%fused_computation.110 | convolution fusion | flops 1642071552 | bytes 28590080 | tf_op jit(solution)/shard_map/sub | solution.py:59
  184.3 17.5 %fusion.1 = (f32[4,2,512]{2,1,0:T(2,128)S(1)}, f32[4,1536,512,2]{2,1,3,0:T(8,128)}) fusion(f32[4,2,512,1536]{2,3,1,0:T(8,128)} %get-tuple-element.28, f32[4,2,512]{2,1,0:T(2,128)S(1)} %get-tuple-element.27, bf16[512,4,2,128]{0,3,2,1:T(8,128)(2,1)} %bitcast.83, bf16[1536,4,128,1]{2,1,0,3:T(4,128)(2,1)} %bitcast.82), kind=kOutput, calls=%fused_computation.3 | convolution fusion | flops 1629483008 | bytes 52985856 | tf_op jit(solution)/shard_map/akgd,ckd->kgac/dot_general | solution.py:61
  201.9 17.0 %fusion.3 = bf16[4,2,512,1536]{2,3,1,0:T(8,128)(2,1)S(1)} fusion(f32[4,1536,512,2]{2,1,3,0:T(8,128)} %get-tuple-element.30, f32[4,2,512]{2,1,0:T(2,128)S(1)} %get-tuple-element.29, f32[4,2,512,1536]{2,3,1,0:T(8,128)} %get-tuple-element.28, f32[4,2,512]{2,1,0:T(2,128)S(1)} %get-tuple-element.27), kind=kLoop, calls=%fused_computation.5 | loop fusion | flops 25165824 | bytes 62947328 | tf_op jit(solution)/shard_map/convert_element_type | solution.py:65
  218.9 2.8 multiply_convert_fusion.1
  221.7 7.0 %fusion.13 = f32[4,128,1536]{2,1,0:T(8,128)} fusion(bf16[512,4,2,128]{0,3,2,1:T(8,128)(2,1)} %bitcast.80, bf16[4,2,512,1536]{2,3,1,0:T(8,128)(2,1)S(1)} %fusion.3), kind=kOutput, calls=%fused_computation.33 | convolution fusion | flops 1611399168 | bytes 16777216 | tf_op jit(solution)/shard_map/kgac,akgd->ckd/dot_general | solution.py:76
  228.7 11.0 %fusion.5 = f32[4,1536,128,1]{1,2,3,0:T(8,128)S(1)} fusion(bf16[512,4,2,128]{0,3,2,1:T(8,128)(2,1)} %bitcast.84, f32[4,2,512,1536]{2,3,1,0:T(8,128)} %get-tuple-element.28, f32[4,2,512]{2,1,0:T(2,128)S(1)} %get-tuple-element.27), kind=kOutput, calls=%fused_computation.10 | convolution fusion | flops 1623195648 | bytes 29376512 | tf_op jit(solution)/shard_map/kgac,akgd->ckd/dot_general | solution.py:79
  239.7 0.6 fusion.10
  240.3 0.2 fusion.69
  240.5 2.2 collective-permute-start.3
  242.7 1.9 collective-permute-start.2
  244.7 3.5 fusion.25
  248.2 3.2 fusion.27
  251.4 3.2 fusion.29
  254.7 13.9 %collective-permute-done.3 = bf16[2,512,512]{1,2,0:T(8,128)(2,1)S(1)} collective-permute-done((bf16[2,512,512]{1,2,0:T(8,128)(2,1)S(1)}, bf16[2,512,512]{1,2,0:T(8,128)(2,1)S(1)}, u32[]{:S(2)}, u32[]{:S(2)}) %collective-permute-start.3) | collective-permute-done | bytes 1048608 | tf_op jit(solution)/shard_map/ppermute | solution.py:19
  268.5 3.7 collective-permute-done.2
  272.2 0.4 fusion.34
  272.7 1.0 slice_bitcast_fusion.1
  273.7 2.2 convolution_add_fusion.3
  275.9 3.3 fusion.19
  279.3 2.9 collective-permute-start.6
  282.1 19.3 %convolution_convert_fusion = bf16[2048,5376]{0,1:T(8,128)(2,1)} fusion(bf16[512,5376]{0,1:T(8,128)(2,1)} %all-gather.2.cloned.1.call-done, bf16[512,512]{0,1:T(8,128)(2,1)} %get-tuple-element.26, bf16[512,512]{0,1:T(8,128)(2,1)} %get-tuple-element.25, bf16[512,1024]{0,1:T(8,128)(2,1)S(1)} %bitcast.88), kind=kOutput, calls=%fused_computation.8 | convolution fusion | flops 11291590656 | bytes 29622272 | tf_op jit(solution)/shard_map/dot_general | solution.py:29
  301.4 12.4 %constant_dynamic-slice_fusion.6 = (bf16[2048,672]{0,1:T(8,128)(2,1)}, bf16[2048,672]{0,1:T(8,128)(2,1)S(1)}, bf16[2048,672]{0,1:T(8,128)(2,1)S(1)}, bf16[2048,6...) fusion(bf16[2048,5376]{0,1:T(8,128)(2,1)} %convolution_convert_fusion, ...), kind=kLoop, calls=%fused_computation.89 | loop fusion | bytes 38535196 | tf_op jit(solution)/shard_map/dynamic_slice | solution.py:148
  313.9 0.1 collective-permute-start.13
  314.0 1.2 collective-permute-start.12
  315.1 2.2 convolution_add_fusion.5
  317.4 2.4 fusion.18
  319.8 0.1 collective-permute-start.5
  319.9 2.2 convolution_add_fusion.7
  322.1 2.2 fusion.17
  324.3 0.3 collective-permute-start.4
  324.6 0.3 collective-permute-start.11
  324.9 85.2 %collective-permute-done.5 = bf16[512,1344]{0,1:T(8,128)(2,1)S(1)} collective-permute-done((bf16[512,1344]{0,1:T(8,128)(2,1)S(1)}, bf16[512,1344]{0,1:T(8,128)(2,1)S(1)}, u32[]{:S(2)}, u32[]{:S(2)}) %collective-permute-start.5) | collective-permute-done | bytes 1376288 | tf_op jit(solution)/shard_map/ppermute | solution.py:138
  410.2 0.9 collective-permute-start.9
  411.1 2.4 collective-permute-start.8
  413.5 16.9 %collective-permute-done.12 = bf16[2048,672]{0,1:T(8,128)(2,1)} collective-permute-done((bf16[2048,672]{0,1:T(8,128)(2,1)S(1)}, bf16[2048,672]{0,1:T(8,128)(2,1)}, u32[]{:S(2)}, u32[]{:S(2)}) %collective-permute-start.12) | collective-permute-done | bytes 2752544 | tf_op jit(solution)/shard_map/ppermute | solution.py:154
  430.4 0.2 collective-permute-start.7
  430.6 3.4 fusion.23
  434.0 2.4 convolution_add_fusion.1
  436.5 3.7 add_convert_fusion
  440.2 149.0 %collective-permute-done.10 = bf16[2048,672]{0,1:T(8,128)(2,1)} collective-permute-done((bf16[2048,672]{0,1:T(8,128)(2,1)}, bf16[2048,672]{0,1:T(8,128)(2,1)}, u32[]{:S(2)}, u32[]{:S(2)}) %collective-permute-start.10) | collective-permute-done | bytes 2752544 | tf_op jit(solution)/shard_map/ppermute | solution.py:154
  589.2 30.1 %collective-permute-done.9 = bf16[2048,672]{0,1:T(8,128)(2,1)} collective-permute-done((bf16[2048,672]{0,1:T(8,128)(2,1)}, bf16[2048,672]{0,1:T(8,128)(2,1)}, u32[]{:S(2)}, u32[]{:S(2)}) %collective-permute-start.9) | collective-permute-done | bytes 2752544 | tf_op jit(solution)/shard_map/ppermute | solution.py:154
  619.3 9.9 %fusion.22 = bf16[672,2048]{1,0:T(8,128)(2,1)S(1)} fusion(bf16[2048,672]{0,1:T(8,128)(2,1)} %collective-permute-done.13, bf16[2048,672]{0,1:T(8,128)(2,1)} %collective-permute-done.12, bf16[2048,672]{0,1:T(8,128)(2,1)} %collective-permute-done.11, bf16[2048,672]{0,1:T(8,128)(2,1)} %collective-permute-done.10, bf16[2048,672]{0,1:T(8,128)(2,1)} %collective-permute-done.9, ...), kind=kLoop, calls=%fused_computation.43 | loop fusion | flops 23396352 | bytes 24772612 | tf_op jit(solution)/shard_map/transpose | solution.py:155
  629.3 1.2 slice.52
  630.5 1.2 fusion.71
  (52 shorter events, 0.2 us)
Async XLA Ops:
  7.2 3.2 copy-start.12
  7.2 103.3 %all-gather.2.cloned.1.call-start = ((), (), s32[]{:S(2)}) async-start(), calls=%async_computation | async-start | bytes 6881280 | tf_op jit(solution)/shard_map/all_gather | solution.py:89
  110.5 7.4 %copy-start.13 = (bf16[512,5376]{0,1:T(8,128)(2,1)S(1)}, bf16[512,5376]{0,1:T(8,128)(2,1)}, u32[]{:S(2)}) copy-start(bf16[512,5376]{0,1:T(8,128)(2,1)} %all-gather.2.cloned.1.call-done) | copy-start | bytes 16515076
  110.5 19.8 %slice-start = ((s8[11010048]{0:T(1024)(128)(4,1)}), s8[4194304]{0:T(1024)(128)(4,1)S(1)}, s32[]{:S(2)}) async-start(s8[11010048]{0:T(1024)(128)(4,1)} %bitcast.90), calls=%async_computation.1 | async-start | bytes 8388608
  110.5 19.8 %slice-start.1 = ((s8[11010048]{0:T(1024)(128)(4,1)}), s8[4194304]{0:T(1024)(128)(4,1)S(1)}, s32[]{:S(2)}) async-start(s8[11010048]{0:T(1024)(128)(4,1)} %bitcast.90), calls=%async_computation.2 | async-start | bytes 8388608
  117.9 12.5 %slice-start.2 = ((s8[11010048]{0:T(1024)(128)(4,1)}), s8[2621440]{0:T(1024)(128)(4,1)S(1)}, s32[]{:S(2)}) async-start(s8[11010048]{0:T(1024)(128)(4,1)} %bitcast.90), calls=%async_computation.3 | async-start | bytes 5242880
  123.7 23.8 %collective-permute-start.1 = (bf16[2,512,512]{2,1,0:T(8,128)(2,1)S(1)}, bf16[2,512,512]{2,1,0:T(8,128)(2,1)}, u32[]{:S(2)}, u32[]{:S(2)}) collective-permute-start(bf16[2,512,512]{2,1,0:T(8,128)(2,1)S(1)} %pad_maximum_fusion.1), channel_id=1, source_target_pairs={{0,4},{4,8},{8,12},{12,16},{16,20},{20,24},{24,28},{1,5},{5,9},{9,... | collective-permute-start | bytes 3145736 | tf_op jit(solution)/shard_map/ppermute | solution.py:19
  127.2 35.0 %collective-permute-start = (bf16[2,512,512]{2,1,0:T(8,128)(2,1)S(1)}, bf16[2,512,512]{2,1,0:T(8,128)(2,1)}, u32[]{:S(2)}, u32[]{:S(2)}) collective-permute-start(bf16[2,512,512]{2,1,0:T(8,128)(2,1)S(1)} %pad_maximum_fusion.1), channel_id=1, source_target_pairs={{0,8},{4,12},{8,16},{12,20},{16,24},{20,28},{1,9},{5,13},{9,17},{1... | collective-permute-start | bytes 3145736 | tf_op jit(solution)/shard_map/ppermute | solution.py:19
  166.7 17.7 %copy-start.1 = (bf16[1536,4,128,1]{0,2,3,1:T(8,128)(2,1)}, bf16[1536,4,128,1]{0,2,3,1:T(8,128)(2,1)S(1)}, u32[]{:S(2)}) copy-start(bf16[1536,4,128,1]{0,2,3,1:T(8,128)(2,1)S(1)} %copy.63) | copy-start | bytes 4718596
  166.7 4.1 copy-start.3
  166.7 4.1 copy-start.11
  201.9 17.0 %copy-start.2 = (bf16[1536,4,128,1]{0,2,3,1:T(8,128)(2,1)S(1)}, bf16[1536,4,128,1]{0,2,3,1:T(8,128)(2,1)}, u32[]{:S(2)}) copy-start(bf16[1536,4,128,1]{0,2,3,1:T(8,128)(2,1)} %copy-done.1) | copy-start | bytes 4718596
  228.7 11.0 %copy-start = (f32[4,128,1536]{2,1,0:T(8,128)S(1)}, f32[4,128,1536]{2,1,0:T(8,128)}, u32[]{:S(2)}) copy-start(f32[4,128,1536]{2,1,0:T(8,128)} %fusion.13) | copy-start | bytes 9437188
  239.7 8.5 %slice-start.3 = ((s8[11010048]{0:T(1024)(128)(4,1)}), s8[2621440]{0:T(1024)(128)(4,1)S(1)}, s32[]{:S(2)}) async-start(s8[11010048]{0:T(1024)(128)(4,1)} %bitcast.92), calls=%async_computation.4 | async-start | bytes 5242880
  239.7 8.5 %slice-start.4 = ((s8[11010048]{0:T(1024)(128)(4,1)}), s8[4194304]{0:T(1024)(128)(4,1)S(1)}, s32[]{:S(2)}) async-start(s8[11010048]{0:T(1024)(128)(4,1)} %bitcast.92), calls=%async_computation.5 | async-start | bytes 8388608
  240.3 4.4 copy-start.10
  240.5 28.0 %collective-permute-start.3 = (bf16[2,512,512]{1,2,0:T(8,128)(2,1)S(1)}, bf16[2,512,512]{1,2,0:T(8,128)(2,1)S(1)}, u32[]{:S(2)}, u32[]{:S(2)}) collective-permute-start(bf16[2,512,512]{1,2,0:T(8,128)(2,1)S(1)} %get-tuple-element.20), channel_id=1, source_target_pairs={{8,0},{12,4},{16,8},{20,12},{24,16},{28,20},{9,1},{13,5},{17,9},{2... | collective-permute-start | bytes 3145736 | tf_op jit(solution)/shard_map/ppermute | solution.py:19
  242.7 29.5 %collective-permute-start.2 = (bf16[2,512,512]{1,2,0:T(8,128)(2,1)S(1)}, bf16[2,512,512]{1,2,0:T(8,128)(2,1)S(1)}, u32[]{:S(2)}, u32[]{:S(2)}) collective-permute-start(bf16[2,512,512]{1,2,0:T(8,128)(2,1)S(1)} %get-tuple-element.19), channel_id=1, source_target_pairs={{4,0},{8,4},{12,8},{16,12},{20,16},{24,20},{28,24},{5,1},{9,5},{13... | collective-permute-start | bytes 3145736 | tf_op jit(solution)/shard_map/ppermute | solution.py:19
  244.7 3.6 slice-start.5
  279.3 45.3 %collective-permute-start.6 = (bf16[512,1344]{0,1:T(8,128)(2,1)}, bf16[512,1344]{0,1:T(8,128)(2,1)S(1)}, u32[]{:S(2)}, u32[]{:S(2)}) collective-permute-start(bf16[512,1344]{0,1:T(8,128)(2,1)} %fusion.19), channel_id=1, source_target_pairs={{0,1},{1,2},{2,3},{3,0},{4,5},{5,6},{6,7},{7,4},{8,9},{9,10},{10,1... | collective-permute-start | bytes 4128776 | tf_op jit(solution)/shard_map/ppermute | solution.py:138
  301.4 13.7 %copy-start.5 = (f32[512,1344]{0,1:T(8,128)S(1)}, f32[512,1344]{0,1:T(8,128)}, u32[]{:S(2)}) copy-start(f32[512,1344]{0,1:T(8,128)} %fusion.27) | copy-start | bytes 8257540
  313.9 97.3 %collective-permute-start.13 = (bf16[2048,672]{0,1:T(8,128)(2,1)S(1)}, bf16[2048,672]{0,1:T(8,128)(2,1)}, u32[]{:S(2)}, u32[]{:S(2)}) collective-permute-start(bf16[2048,672]{0,1:T(8,128)(2,1)S(1)} %get-tuple-element.13), channel_id=1, source_target_pairs={{0,4},{4,8},{8,12},{12,16},{16,20},{20,24},{24,28},{28,0},{1,5},{5... | collective-permute-start | bytes 8257544 | tf_op jit(solution)/shard_map/ppermute | solution.py:154
  314.0 116.4 %collective-permute-start.12 = (bf16[2048,672]{0,1:T(8,128)(2,1)S(1)}, bf16[2048,672]{0,1:T(8,128)(2,1)}, u32[]{:S(2)}, u32[]{:S(2)}) collective-permute-start(bf16[2048,672]{0,1:T(8,128)(2,1)S(1)} %get-tuple-element.14), channel_id=1, source_target_pairs={{0,8},{4,12},{8,16},{12,20},{16,24},{20,28},{24,0},{28,4},{1,9},{5... | collective-permute-start | bytes 8257544 | tf_op jit(solution)/shard_map/ppermute | solution.py:154
  317.4 2.5 copy-start.4
  319.8 90.4 %collective-permute-start.5 = (bf16[512,1344]{0,1:T(8,128)(2,1)S(1)}, bf16[512,1344]{0,1:T(8,128)(2,1)S(1)}, u32[]{:S(2)}, u32[]{:S(2)}) collective-permute-start(bf16[512,1344]{0,1:T(8,128)(2,1)S(1)} %fusion.18), channel_id=1, source_target_pairs={{0,2},{1,3},{2,0},{3,1},{4,6},{5,7},{6,4},{7,5},{8,10},{9,11},{10,... | collective-permute-start | bytes 4128776 | tf_op jit(solution)/shard_map/ppermute | solution.py:138
  324.3 85.8 %collective-permute-start.4 = (bf16[512,1344]{0,1:T(8,128)(2,1)S(1)}, bf16[512,1344]{0,1:T(8,128)(2,1)S(1)}, u32[]{:S(2)}, u32[]{:S(2)}) collective-permute-start(bf16[512,1344]{0,1:T(8,128)(2,1)S(1)} %fusion.17), channel_id=1, source_target_pairs={{0,3},{1,0},{2,1},{3,2},{4,7},{5,4},{6,5},{7,6},{8,11},{9,8},{10,9... | collective-permute-start | bytes 4128776 | tf_op jit(solution)/shard_map/ppermute | solution.py:138
  324.6 115.6 %collective-permute-start.11 = (bf16[2048,672]{0,1:T(8,128)(2,1)}, bf16[2048,672]{0,1:T(8,128)(2,1)}, u32[]{:S(2)}, u32[]{:S(2)}) collective-permute-start(bf16[2048,672]{0,1:T(8,128)(2,1)} %get-tuple-element.15), channel_id=1, source_target_pairs={{0,12},{4,16},{8,20},{12,24},{16,28},{20,0},{24,4},{28,8},{1,13},{... | collective-permute-start | bytes 8257544 | tf_op jit(solution)/shard_map/ppermute | solution.py:154
  410.1 20.2 %copy-start.6 = (bf16[512,1344]{0,1:T(8,128)(2,1)}, bf16[512,1344]{0,1:T(8,128)(2,1)S(1)}, u32[]{:S(2)}) copy-start(bf16[512,1344]{0,1:T(8,128)(2,1)S(1)} %collective-permute-done.5) | copy-start | bytes 4128772
  410.1 179.0 %collective-permute-start.10 = (bf16[2048,672]{0,1:T(8,128)(2,1)}, bf16[2048,672]{0,1:T(8,128)(2,1)}, u32[]{:S(2)}, u32[]{:S(2)}) collective-permute-start(bf16[2048,672]{0,1:T(8,128)(2,1)} %get-tuple-element.16), channel_id=1, source_target_pairs={{0,16},{4,20},{8,24},{12,28},{16,0},{20,4},{24,8},{28,12},{1,17},{... | collective-permute-start | bytes 8257544 | tf_op jit(solution)/shard_map/ppermute | solution.py:154
  410.2 20.2 %copy-start.8 = (bf16[512,1344]{0,1:T(8,128)(2,1)}, bf16[512,1344]{0,1:T(8,128)(2,1)S(1)}, u32[]{:S(2)}) copy-start(bf16[512,1344]{0,1:T(8,128)(2,1)S(1)} %collective-permute-done.4) | copy-start | bytes 4128772
  410.2 209.2 %collective-permute-start.9 = (bf16[2048,672]{0,1:T(8,128)(2,1)}, bf16[2048,672]{0,1:T(8,128)(2,1)}, u32[]{:S(2)}, u32[]{:S(2)}) collective-permute-start(bf16[2048,672]{0,1:T(8,128)(2,1)} %get-tuple-element.17), channel_id=1, source_target_pairs={{0,20},{4,24},{8,28},{12,0},{16,4},{20,8},{24,12},{28,16},{1,21},{... | collective-permute-start | bytes 8257544 | tf_op jit(solution)/shard_map/ppermute | solution.py:154
  411.1 208.2 %collective-permute-start.8 = (bf16[2048,672]{0,1:T(8,128)(2,1)}, bf16[2048,672]{0,1:T(8,128)(2,1)}, u32[]{:S(2)}, u32[]{:S(2)}) collective-permute-start(bf16[2048,672]{0,1:T(8,128)(2,1)} %get-tuple-element.18), channel_id=1, source_target_pairs={{0,24},{4,28},{8,0},{12,4},{16,8},{20,12},{24,16},{28,20},{1,25},{... | collective-permute-start | bytes 8257544 | tf_op jit(solution)/shard_map/ppermute | solution.py:154
  430.4 188.9 %collective-permute-start.7 = (bf16[2048,672]{0,1:T(8,128)(2,1)}, bf16[2048,672]{0,1:T(8,128)(2,1)}, u32[]{:S(2)}, u32[]{:S(2)}) collective-permute-start(bf16[2048,672]{0,1:T(8,128)(2,1)} %get-tuple-element.12), channel_id=1, source_target_pairs={{0,28},{4,0},{8,4},{12,8},{16,12},{20,16},{24,20},{28,24},{1,29},{... | collective-permute-start | bytes 8257544 | tf_op jit(solution)/shard_map/ppermute | solution.py:154
  434.0 2.4 copy-start.7
  434.0 2.4 copy-start.9
Sparse Core Ops, SparseCore 0:
  9.6 100.8 all-gather.1
where the time goes:
time: 646 us; the launch traced here: 639 us
  waiting for transfers between devices  421 us (65%)
  matrix products  124 us (19%)
  other arithmetic  32.4 us (5%)
  local copies, waits for them, and re-layouts  27.2 us (4%)
  starting transfers between devices  19 us (3%)
  between operations  14.9 us (2%)
    ppermute x7, waiting for transfers between devices, per_device(): weight_sum = weight_sum + lax.ppermute(sent, SEQ, pairs).astype(jnp.float32)  196 us
    all_gather x1, waiting for transfers between devices, per_device(): gathered = lax.all_gather(tokens, 'head', axis=1, tiled=True)  97.3 us
    ppermute x3, waiting for transfers between devices, per_device(): got = lax.ppermute(sent, 'head', pairs).astype(jnp.float32)  85.2 us
    ppermute x4, waiting for transfers between devices, passed_along(): return lax.ppermute(x, axis, pairs)  41.7 us
    dot_general x12, matrix products, contract_last(): lax.dot_general(left, right, (((1,), (1,)), ((), ())), preferred_element_...  34 us
    dot_general x1, matrix products, contract_first(): lax.dot_general(left, right, (((0,), (0,)), ((), ())), preferred_element_...  19.3 us
    dot_general x1, matrix products, attend(): jnp.einsum('akgd,ckd->kgac', grad_four, value_three, preferred_element_ty...  17.5 us
    convert_element_type x1, other arithmetic, attend(): dscores = (probs * (dprobs - center)).astype(jnp.bfloat16)  17 us
  transfers between devices with their start and end apart: 15, of which 9 were waited for; matrix products, arithmetic and copies ran while one was open for 11% of the time, Pallas kernels for 0%

commit v1 on v0

--- a/solution.py
+++ b/solution.py
@@ -86,7 +86,24 @@
     tok_rows = tokens.shape[0]
     hop_count = HOPS
     margin = hop_count * tok_rows
-    gathered = lax.all_gather(tokens, "head", axis=1, tiled=True)
+    ways, here, step = (lax.axis_size("head"), lax.axis_index("head"), tokens.shape[1])
+    lengths = [n * ways if d == 1 else n for d, n in enumerate(tokens.shape)]
+    gathered = lax.dynamic_update_slice_in_dim(
+        jnp.zeros(lengths, tokens.dtype), tokens, here * step, axis=1
+    )
+    going_up = going_down = tokens
+    for far in range(1, ways // 2 + 1):
+        going_up = lax.ppermute(going_up, "head", [(d, (d + 1) % ways) for d in range(ways)])
+        gathered = lax.dynamic_update_slice_in_dim(
+            gathered, going_up, (here - far) % ways * step, axis=1
+        )
+        if 2 * far < ways:
+            going_down = lax.ppermute(
+                going_down, "head", [(d, (d - 1) % ways) for d in range(ways)]
+            )
+            gathered = lax.dynamic_update_slice_in_dim(
+                gathered, going_down, (here + far) % ways * step, axis=1
+            )
     queries = jnp.dot(gathered, query_weight, preferred_element_type=jnp.float32).astype(
         jnp.bfloat16
     )

time: 646 us -> 616 us (0.954)
  waiting for transfers between devices: 421 us -> 400 us
  between operations: 14.9 us -> 1.68 us
  matrix products: 124 us -> 117 us
    all_gather x1 -> x0, waiting for transfers between devices: 97.3 us -> none  [per_device(): gathered = lax.all_gather(tokens, 'head', axis=1, tiled=True)]
    ppermute x0 -> x3, waiting for transfers between devices: none -> 76.1 us  [the longest x2 55.9 us: per_device(): lax.ppermute(going_up, 'head', [(d, (d + 1) % ways) for d in range(ways)])]
  transfers between devices with their start and end apart: 15 -> 17, of which waited for: 9 -> 11; matrix products, arithmetic and copies ran while one was open for 11% -> 13% of each run, Pallas kernels for 0% -> 0%
where the time goes in v1:
time: 616 us; the launch traced here: 608 us
  waiting for transfers between devices  400 us (65%)
  matrix products  117 us (19%)
  other arithmetic  33.1 us (5%)
  local copies, waits for them, and re-layouts  32.2 us (5%)
  starting transfers between devices  23.9 us (4%)
    ppermute x7, waiting for transfers between devices, per_device(): weight_sum = weight_sum + lax.ppermute(sent, SEQ, pairs).astype(jnp.float32)  196 us
    ppermute x3, waiting for transfers between devices, per_device(): got = lax.ppermute(sent, 'head', pairs).astype(jnp.float32)  86.3 us
    ppermute x2, waiting for transfers between devices, per_device(): lax.ppermute(going_up, 'head', [(d, (d + 1) % ways) for d in range(ways)])  55.9 us
    ppermute x4, waiting for transfers between devices, passed_along(): return lax.ppermute(x, axis, pairs)  42 us
    dot_general x12, matrix products, contract_last(): lax.dot_general(left, right, (((1,), (1,)), ((), ())), preferred_element_...  34 us
    ppermute x1, waiting for transfers between devices, per_device(): lax.ppermute(going_down, 'head', [(d, (d - 1) % ways) for d in range(ways)])  20.2 us
    dot_general x1, matrix products, contract_first(): lax.dot_general(left, right, (((0,), (0,)), ((), ())), preferred_element_...  19.3 us
    dot_general x1, matrix products, attend(): jnp.einsum('akgd,ckd->kgac', grad_four, value_three, preferred_element_ty...  17.5 us
  transfers between devices with their start and end apart: 17, of which 11 were waited for; matrix products, arithmetic and copies ran while one was open for 13% of the time, Pallas kernels for 0%

profile of v1, /device:TPU:27, one launch (start us, length us, event | category | flops | bytes accessed | tf_op | source)
XLA Modules:
  0.0 608.4 jit_solution(9467733832261084733)
XLA Ops:
  0.7 1.5 collective-permute-start.1
  2.2 0.8 pad_dynamic-slice_fusion
  2.9 29.2 %collective-permute-done = bf16[512,1344]{0,1:T(8,128)(2,1)S(1)} collective-permute-done((bf16[512,1344]{0,1:T(8,128)(2,1)}, bf16[512,1344]{0,1:T(8,128)(2,1)S(1)}, u32[]{:S(2)}, u32[]{:S(2)}) %collective-permute-start) | collective-permute-done | bytes 1376288 | tf_op jit(solution)/shard_map/ppermute | solution.py:96
  32.2 1.7 collective-permute-start.2
  33.9 0.8 dynamic_slice.66
  34.6 2.3 copy.77
  36.9 0.4 broadcast_in_dim.24
  37.3 1.0 copy-done.11
  38.4 2.7 fusion.16
  41.2 20.2 %collective-permute-done.1 = bf16[512,1344]{0,1:T(8,128)(2,1)} collective-permute-done((bf16[512,1344]{0,1:T(8,128)(2,1)}, bf16[512,1344]{0,1:T(8,128)(2,1)}, u32[]{:S(2)}, u32[]{:S(2)}) %collective-permute-start.1) | collective-permute-done | bytes 1376288 | tf_op jit(solution)/shard_map/ppermute | solution.py:101
  61.4 1.5 constant_dynamic-update-slice_fusion.1
  62.8 26.7 %collective-permute-done.2 = bf16[512,1344]{0,1:T(8,128)(2,1)} collective-permute-done((bf16[512,1344]{0,1:T(8,128)(2,1)S(1)}, bf16[512,1344]{0,1:T(8,128)(2,1)}, u32[]{:S(2)}, u32[]{:S(2)}) %collective-permute-start.2) | collective-permute-done | bytes 1376288 | tf_op jit(solution)/shard_map/ppermute | solution.py:96
  89.5 1.6 constant_dynamic-update-slice_fusion
  91.2 3.0 fusion.53
  94.3 3.0 fusion.52
  97.4 6.1 collective-permute-start.4
  103.5 3.1 collective-permute-start.3
  106.7 5.9 convolution_convert_fusion.1
  112.6 1.5 copy.76
  114.1 9.8 %collective-permute-done.4 = bf16[2,512,512]{2,1,0:T(8,128)(2,1)} collective-permute-done((bf16[2,512,512]{2,1,0:T(8,128)(2,1)S(1)}, bf16[2,512,512]{2,1,0:T(8,128)(2,1)}, u32[]{:S(2)}, u32[]{:S(2)}) %collective-permute-start.4) | collective-permute-done | bytes 1048608 | tf_op jit(solution)/shard_map/ppermute | solution.py:19
  123.9 14.6 %collective-permute-done.3 = bf16[2,512,512]{2,1,0:T(8,128)(2,1)} collective-permute-done((bf16[2,512,512]{2,1,0:T(8,128)(2,1)S(1)}, bf16[2,512,512]{2,1,0:T(8,128)(2,1)}, u32[]{:S(2)}, u32[]{:S(2)}) %collective-permute-start.3) | collective-permute-done | bytes 1048608 | tf_op jit(solution)/shard_map/ppermute | solution.py:19
  138.5 1.7 maximum_maximum_fusion
  140.2 1.4 fusion.70
  141.6 0.4 reshape_squeeze.6
  142.0 1.0 copy.63
  143.0 4.0 reshape_squeeze.7
  147.1 13.6 %fusion.72 = (f32[4,2,512]{2,1,0:T(2,128)S(1)}, f32[4,2,512,1536]{2,3,1,0:T(8,128)}) fusion(pred[512,1536]{0,1:T(8,128)(4,1)S(1)} %copy-done.13, bf16[1536,4,128,1]{0,2,3,1:T(8,128)(2,1)S(1)} %copy.63, bf16[512,4,2,128]{0,3,2,1:T(8,128)(2,1)S(1)} %bitcast.85), kind=kOutput, calls=%fused_computation.114 | convolution fusion | flops 1642071552 | bytes 28590080 | tf_op jit(solution)/shard_map/sub | solution.py:59
  160.6 17.5 %fusion.1 = (f32[4,2,512]{2,1,0:T(2,128)S(1)}, f32[4,1536,512,2]{2,1,3,0:T(8,128)}) fusion(f32[4,2,512,1536]{2,3,1,0:T(8,128)} %get-tuple-element.28, f32[4,2,512]{2,1,0:T(2,128)S(1)} %get-tuple-element.27, bf16[512,4,2,128]{0,3,2,1:T(8,128)(2,1)} %bitcast.87, bf16[1536,4,128,1]{2,1,0,3:T(4,128)(2,1)} %bitcast.86), kind=kOutput, calls=%fused_computation.3 | convolution fusion | flops 1629483008 | bytes 52985856 | tf_op jit(solution)/shard_map/akgd,ckd->kgac/dot_general | solution.py:61
  178.1 17.0 %fusion.3 = bf16[4,2,512,1536]{2,3,1,0:T(8,128)(2,1)S(1)} fusion(f32[4,1536,512,2]{2,1,3,0:T(8,128)} %get-tuple-element.30, f32[4,2,512]{2,1,0:T(2,128)S(1)} %get-tuple-element.29, f32[4,2,512,1536]{2,3,1,0:T(8,128)} %get-tuple-element.28, f32[4,2,512]{2,1,0:T(2,128)S(1)} %get-tuple-element.27), kind=kLoop, calls=%fused_computation.5 | loop fusion | flops 25165824 | bytes 62947328 | tf_op jit(solution)/shard_map/convert_element_type | solution.py:65
  195.1 2.9 multiply_convert_fusion.1
  197.9 7.0 %fusion.13 = f32[4,128,1536]{2,1,0:T(8,128)} fusion(bf16[512,4,2,128]{0,3,2,1:T(8,128)(2,1)} %bitcast.84, bf16[4,2,512,1536]{2,3,1,0:T(8,128)(2,1)S(1)} %fusion.3), kind=kOutput, calls=%fused_computation.33 | convolution fusion | flops 1611399168 | bytes 16777216 | tf_op jit(solution)/shard_map/kgac,akgd->ckd/dot_general | solution.py:76
  204.9 11.0 %fusion.5 = f32[4,1536,128,1]{1,2,3,0:T(8,128)S(1)} fusion(bf16[512,4,2,128]{0,3,2,1:T(8,128)(2,1)} %bitcast.88, f32[4,2,512,1536]{2,3,1,0:T(8,128)} %get-tuple-element.28, f32[4,2,512]{2,1,0:T(2,128)S(1)} %get-tuple-element.27), kind=kOutput, calls=%fused_computation.10 | convolution fusion | flops 1623195648 | bytes 29376512 | tf_op jit(solution)/shard_map/kgac,akgd->ckd/dot_general | solution.py:79
  216.0 0.6 fusion.10
  216.8 2.2 collective-permute-start.6
  219.0 1.9 collective-permute-start.5
  220.9 3.5 fusion.25
  224.5 3.2 fusion.27
  227.7 3.2 fusion.29
  230.9 13.9 %collective-permute-done.6 = bf16[2,512,512]{1,2,0:T(8,128)(2,1)S(1)} collective-permute-done((bf16[2,512,512]{1,2,0:T(8,128)(2,1)S(1)}, bf16[2,512,512]{1,2,0:T(8,128)(2,1)S(1)}, u32[]{:S(2)}, u32[]{:S(2)}) %collective-permute-start.6) | collective-permute-done | bytes 1048608 | tf_op jit(solution)/shard_map/ppermute | solution.py:19
  244.8 3.6 collective-permute-done.5
  248.5 0.4 fusion.34
  248.9 1.0 slice_bitcast_fusion.1
  249.9 2.2 convolution_add_fusion.3
  252.2 3.3 fusion.19
  255.5 1.9 collective-permute-start.9
  257.3 19.3 %convolution_convert_fusion = bf16[2048,5376]{0,1:T(8,128)(2,1)} fusion(bf16[512,5376]{0,1:T(8,128)(2,1)} %copy-done.3, bf16[512,512]{0,1:T(8,128)(2,1)} %get-tuple-element.26, bf16[512,512]{0,1:T(8,128)(2,1)} %get-tuple-element.25, bf16[512,1024]{0,1:T(8,128)(2,1)S(1)} %bitcast.92), kind=kOutput, calls=%fused_computation.8 | convolution fusion | flops 11291590656 | bytes 29622272 | tf_op jit(solution)/shard_map/dot_general | solution.py:29
  276.7 12.4 %constant_dynamic-slice_fusion.6 = (bf16[2048,672]{0,1:T(8,128)(2,1)}, bf16[2048,672]{0,1:T(8,128)(2,1)S(1)}, bf16[2048,672]{0,1:T(8,128)(2,1)S(1)}, bf16[2048,6...) fusion(bf16[2048,5376]{0,1:T(8,128)(2,1)} %convolution_convert_fusion, ...), kind=kLoop, calls=%fused_computation.89 | loop fusion | bytes 38535196 | tf_op jit(solution)/shard_map/dynamic_slice | solution.py:165
  289.2 1.2 collective-permute-start.15
  290.4 2.2 convolution_add_fusion.5
  292.7 2.4 fusion.18
  295.1 2.2 convolution_add_fusion.7
  297.4 2.2 fusion.17
  300.2 86.3 %collective-permute-done.8 = bf16[512,1344]{0,1:T(8,128)(2,1)S(1)} collective-permute-done((bf16[512,1344]{0,1:T(8,128)(2,1)S(1)}, bf16[512,1344]{0,1:T(8,128)(2,1)S(1)}, u32[]{:S(2)}, u32[]{:S(2)}) %collective-permute-start.8) | collective-permute-done | bytes 1376288 | tf_op jit(solution)/shard_map/ppermute | solution.py:155
  386.5 0.9 collective-permute-start.12
  387.4 2.4 collective-permute-start.11
  389.8 15.8 %collective-permute-done.15 = bf16[2048,672]{0,1:T(8,128)(2,1)} collective-permute-done((bf16[2048,672]{0,1:T(8,128)(2,1)S(1)}, bf16[2048,672]{0,1:T(8,128)(2,1)}, u32[]{:S(2)}, u32[]{:S(2)}) %collective-permute-start.15) | collective-permute-done | bytes 2752544 | tf_op jit(solution)/shard_map/ppermute | solution.py:171
  405.9 3.4 fusion.23
  409.3 2.4 convolution_add_fusion.1
  411.7 3.7 add_convert_fusion
  415.4 150.1 %collective-permute-done.13 = bf16[2048,672]{0,1:T(8,128)(2,1)} collective-permute-done((bf16[2048,672]{0,1:T(8,128)(2,1)}, bf16[2048,672]{0,1:T(8,128)(2,1)}, u32[]{:S(2)}, u32[]{:S(2)}) %collective-permute-start.13) | collective-permute-done | bytes 2752544 | tf_op jit(solution)/shard_map/ppermute | solution.py:171
  565.5 30.1 %collective-permute-done.12 = bf16[2048,672]{0,1:T(8,128)(2,1)} collective-permute-done((bf16[2048,672]{0,1:T(8,128)(2,1)}, bf16[2048,672]{0,1:T(8,128)(2,1)}, u32[]{:S(2)}, u32[]{:S(2)}) %collective-permute-start.12) | collective-permute-done | bytes 2752544 | tf_op jit(solution)/shard_map/ppermute | solution.py:171
  595.6 9.9 %fusion.22 = bf16[672,2048]{1,0:T(8,128)(2,1)S(1)} fusion(bf16[2048,672]{0,1:T(8,128)(2,1)} %collective-permute-done.16, bf16[2048,672]{0,1:T(8,128)(2,1)} %collective-permute-done.15, bf16[2048,672]{0,1:T(8,128)(2,1)} %collective-permute-done.14, bf16[2048,672]{0,1:T(8,128)(2,1)} %collective-permute-done.13, bf16[2048,672]{0,1:T(8,128)(2,1)} %collective-permute-done.12, ...), kind=kLoop, calls=%fused_computation.43 | loop fusion | flops 23396352 | bytes 24772612 | tf_op jit(solution)/shard_map/transpose | solution.py:172
  605.6 1.2 slice.52
  606.8 1.2 fusion.71
  (70 shorter events, 1.8 us)
Async XLA Ops:
  0.6 31.5 %collective-permute-start = (bf16[512,1344]{0,1:T(8,128)(2,1)}, bf16[512,1344]{0,1:T(8,128)(2,1)S(1)}, u32[]{:S(2)}, u32[]{:S(2)}) collective-permute-start(bf16[512,1344]{0,1:T(8,128)(2,1)} %param.6), channel_id=1, source_target_pairs={{0,1},{1,2},{2,3},{3,0},{4,5},{5,6},{6,7},{7,4},{8,9},{9,10},{10,1... | collective-permute-start | bytes 4128776 | tf_op jit(solution)/shard_map/ppermute | solution.py:96
  0.7 60.7 %collective-permute-start.1 = (bf16[512,1344]{0,1:T(8,128)(2,1)}, bf16[512,1344]{0,1:T(8,128)(2,1)}, u32[]{:S(2)}, u32[]{:S(2)}) collective-permute-start(bf16[512,1344]{0,1:T(8,128)(2,1)} %param.6), channel_id=1, source_target_pairs={{0,3},{1,0},{2,1},{3,2},{4,7},{5,4},{6,5},{7,6},{8,11},{9,8},{10,9... | collective-permute-start | bytes 4128776 | tf_op jit(solution)/shard_map/ppermute | solution.py:101
  32.2 57.4 %collective-permute-start.2 = (bf16[512,1344]{0,1:T(8,128)(2,1)S(1)}, bf16[512,1344]{0,1:T(8,128)(2,1)}, u32[]{:S(2)}, u32[]{:S(2)}) collective-permute-start(bf16[512,1344]{0,1:T(8,128)(2,1)S(1)} %collective-permute-done), channel_id=1, source_target_pairs={{0,1},{1,2},{2,3},{3,0},{4,5},{5,6},{6,7},{7,4},{8,9},{9,10},{10,1... | collective-permute-start | bytes 4128776 | tf_op jit(solution)/shard_map/ppermute | solution.py:96
  36.9 1.3 copy-start.11
  38.2 52.9 %slice-start = ((s8[5505024]{0:T(1024)(128)(4,1)}), s8[4194304]{0:T(1024)(128)(4,1)S(1)}, s32[]{:S(2)}) async-start(s8[5505024]{0:T(1024)(128)(4,1)} %bitcast.80), calls=%async_computation | async-start | bytes 8388608
  41.0 50.1 %slice-start.1 = ((s8[5505024]{0:T(1024)(128)(4,1)}), s8[1310720]{0:T(1024)(128)(4,1)S(1)}, s32[]{:S(2)}) async-start(s8[5505024]{0:T(1024)(128)(4,1)} %bitcast.80), calls=%async_computation.1 | async-start | bytes 2621440
  89.5 4.7 slice-start.2
  91.2 15.5 %copy-start.3 = (bf16[512,5376]{0,1:T(8,128)(2,1)}, bf16[512,5376]{0,1:T(8,128)(2,1)S(1)}, u32[]{:S(2)}) copy-start(bf16[512,5376]{0,1:T(8,128)(2,1)S(1)} %constant_dynamic-update-slice_fusion) | copy-start | bytes 16515076
  91.2 3.1 slice-start.3
  91.2 15.4 %slice-start.4 = ((s8[11010048]{0:T(1024)(128)(4,1)}), s8[4194304]{0:T(1024)(128)(4,1)S(1)}, s32[]{:S(2)}) async-start(s8[11010048]{0:T(1024)(128)(4,1)} %bitcast.94), calls=%async_computation.4 | async-start | bytes 8388608
  91.2 15.4 %slice-start.5 = ((s8[11010048]{0:T(1024)(128)(4,1)}), s8[4194304]{0:T(1024)(128)(4,1)S(1)}, s32[]{:S(2)}) async-start(s8[11010048]{0:T(1024)(128)(4,1)} %bitcast.94), calls=%async_computation.5 | async-start | bytes 8388608
  94.3 12.4 %slice-start.6 = ((s8[11010048]{0:T(1024)(128)(4,1)}), s8[2621440]{0:T(1024)(128)(4,1)S(1)}, s32[]{:S(2)}) async-start(s8[11010048]{0:T(1024)(128)(4,1)} %bitcast.94), calls=%async_computation.6 | async-start | bytes 5242880
  97.4 26.4 %collective-permute-start.4 = (bf16[2,512,512]{2,1,0:T(8,128)(2,1)S(1)}, bf16[2,512,512]{2,1,0:T(8,128)(2,1)}, u32[]{:S(2)}, u32[]{:S(2)}) collective-permute-start(bf16[2,512,512]{2,1,0:T(8,128)(2,1)S(1)} %pad_maximum_fusion.1), channel_id=1, source_target_pairs={{0,4},{4,8},{8,12},{12,16},{16,20},{20,24},{24,28},{1,5},{5,9},{9,... | collective-permute-start | bytes 3145736 | tf_op jit(solution)/shard_map/ppermute | solution.py:19
  103.5 35.0 %collective-permute-start.3 = (bf16[2,512,512]{2,1,0:T(8,128)(2,1)S(1)}, bf16[2,512,512]{2,1,0:T(8,128)(2,1)}, u32[]{:S(2)}, u32[]{:S(2)}) collective-permute-start(bf16[2,512,512]{2,1,0:T(8,128)(2,1)S(1)} %pad_maximum_fusion.1), channel_id=1, source_target_pairs={{0,8},{4,12},{8,16},{12,20},{16,24},{20,28},{1,9},{5,13},{9,17},{1... | collective-permute-start | bytes 3145736 | tf_op jit(solution)/shard_map/ppermute | solution.py:19
  143.0 17.6 %copy-start.1 = (bf16[1536,4,128,1]{0,2,3,1:T(8,128)(2,1)}, bf16[1536,4,128,1]{0,2,3,1:T(8,128)(2,1)S(1)}, u32[]{:S(2)}) copy-start(bf16[1536,4,128,1]{0,2,3,1:T(8,128)(2,1)S(1)} %copy.63) | copy-start | bytes 4718596
  143.0 4.1 copy-start.4
  143.0 4.0 copy-start.13
  178.1 17.0 %copy-start.2 = (bf16[1536,4,128,1]{0,2,3,1:T(8,128)(2,1)S(1)}, bf16[1536,4,128,1]{0,2,3,1:T(8,128)(2,1)}, u32[]{:S(2)}) copy-start(bf16[1536,4,128,1]{0,2,3,1:T(8,128)(2,1)} %copy-done.1) | copy-start | bytes 4718596
  204.9 11.0 %copy-start = (f32[4,128,1536]{2,1,0:T(8,128)S(1)}, f32[4,128,1536]{2,1,0:T(8,128)}, u32[]{:S(2)}) copy-start(f32[4,128,1536]{2,1,0:T(8,128)} %fusion.13) | copy-start | bytes 9437188
  216.0 8.5 %slice-start.7 = ((s8[11010048]{0:T(1024)(128)(4,1)}), s8[2621440]{0:T(1024)(128)(4,1)S(1)}, s32[]{:S(2)}) async-start(s8[11010048]{0:T(1024)(128)(4,1)} %bitcast.96), calls=%async_computation.7 | async-start | bytes 5242880
  216.0 8.5 %slice-start.8 = ((s8[11010048]{0:T(1024)(128)(4,1)}), s8[4194304]{0:T(1024)(128)(4,1)S(1)}, s32[]{:S(2)}) async-start(s8[11010048]{0:T(1024)(128)(4,1)} %bitcast.96), calls=%async_computation.8 | async-start | bytes 8388608
  216.6 4.4 copy-start.12
  216.8 28.0 %collective-permute-start.6 = (bf16[2,512,512]{1,2,0:T(8,128)(2,1)S(1)}, bf16[2,512,512]{1,2,0:T(8,128)(2,1)S(1)}, u32[]{:S(2)}, u32[]{:S(2)}) collective-permute-start(bf16[2,512,512]{1,2,0:T(8,128)(2,1)S(1)} %get-tuple-element.20), channel_id=1, source_target_pairs={{8,0},{12,4},{16,8},{20,12},{24,16},{28,20},{9,1},{13,5},{17,9},{2... | collective-permute-start | bytes 3145736 | tf_op jit(solution)/shard_map/ppermute | solution.py:19
  219.0 29.5 %collective-permute-start.5 = (bf16[2,512,512]{1,2,0:T(8,128)(2,1)S(1)}, bf16[2,512,512]{1,2,0:T(8,128)(2,1)S(1)}, u32[]{:S(2)}, u32[]{:S(2)}) collective-permute-start(bf16[2,512,512]{1,2,0:T(8,128)(2,1)S(1)} %get-tuple-element.19), channel_id=1, source_target_pairs={{4,0},{8,4},{12,8},{16,12},{20,16},{24,20},{28,24},{5,1},{9,5},{13... | collective-permute-start | bytes 3145736 | tf_op jit(solution)/shard_map/ppermute | solution.py:19
  220.9 3.6 slice-start.9
  255.5 44.4 %collective-permute-start.9 = (bf16[512,1344]{0,1:T(8,128)(2,1)}, bf16[512,1344]{0,1:T(8,128)(2,1)S(1)}, u32[]{:S(2)}, u32[]{:S(2)}) collective-permute-start(bf16[512,1344]{0,1:T(8,128)(2,1)} %fusion.19), channel_id=1, source_target_pairs={{0,1},{1,2},{2,3},{3,0},{4,5},{5,6},{6,7},{7,4},{8,9},{9,10},{10,1... | collective-permute-start | bytes 4128776 | tf_op jit(solution)/shard_map/ppermute | solution.py:155
  276.7 13.7 %copy-start.6 = (f32[512,1344]{0,1:T(8,128)S(1)}, f32[512,1344]{0,1:T(8,128)}, u32[]{:S(2)}) copy-start(f32[512,1344]{0,1:T(8,128)} %fusion.27) | copy-start | bytes 8257540
  289.1 98.3 %collective-permute-start.16 = (bf16[2048,672]{0,1:T(8,128)(2,1)S(1)}, bf16[2048,672]{0,1:T(8,128)(2,1)}, u32[]{:S(2)}, u32[]{:S(2)}) collective-permute-start(bf16[2048,672]{0,1:T(8,128)(2,1)S(1)} %get-tuple-element.13), channel_id=1, source_target_pairs={{0,4},{4,8},{8,12},{12,16},{16,20},{20,24},{24,28},{28,0},{1,5},{5... | collective-permute-start | bytes 8257544 | tf_op jit(solution)/shard_map/ppermute | solution.py:171
  289.2 116.4 %collective-permute-start.15 = (bf16[2048,672]{0,1:T(8,128)(2,1)S(1)}, bf16[2048,672]{0,1:T(8,128)(2,1)}, u32[]{:S(2)}, u32[]{:S(2)}) collective-permute-start(bf16[2048,672]{0,1:T(8,128)(2,1)S(1)} %get-tuple-element.14), channel_id=1, source_target_pairs={{0,8},{4,12},{8,16},{12,20},{16,24},{20,28},{24,0},{28,4},{1,9},{5... | collective-permute-start | bytes 8257544 | tf_op jit(solution)/shard_map/ppermute | solution.py:171
  292.7 2.5 copy-start.5
  295.1 91.4 %collective-permute-start.8 = (bf16[512,1344]{0,1:T(8,128)(2,1)S(1)}, bf16[512,1344]{0,1:T(8,128)(2,1)S(1)}, u32[]{:S(2)}, u32[]{:S(2)}) collective-permute-start(bf16[512,1344]{0,1:T(8,128)(2,1)S(1)} %fusion.18), channel_id=1, source_target_pairs={{0,2},{1,3},{2,0},{3,1},{4,6},{5,7},{6,4},{7,5},{8,10},{9,11},{10,... | collective-permute-start | bytes 4128776 | tf_op jit(solution)/shard_map/ppermute | solution.py:155
  299.6 86.8 %collective-permute-start.7 = (bf16[512,1344]{0,1:T(8,128)(2,1)S(1)}, bf16[512,1344]{0,1:T(8,128)(2,1)S(1)}, u32[]{:S(2)}, u32[]{:S(2)}) collective-permute-start(bf16[512,1344]{0,1:T(8,128)(2,1)S(1)} %fusion.17), channel_id=1, source_target_pairs={{0,3},{1,0},{2,1},{3,2},{4,7},{5,4},{6,5},{7,6},{8,11},{9,8},{10,9... | collective-permute-start | bytes 4128776 | tf_op jit(solution)/shard_map/ppermute | solution.py:155
  299.9 115.5 %collective-permute-start.14 = (bf16[2048,672]{0,1:T(8,128)(2,1)}, bf16[2048,672]{0,1:T(8,128)(2,1)}, u32[]{:S(2)}, u32[]{:S(2)}) collective-permute-start(bf16[2048,672]{0,1:T(8,128)(2,1)} %get-tuple-element.15), channel_id=1, source_target_pairs={{0,12},{4,16},{8,20},{12,24},{16,28},{20,0},{24,4},{28,8},{1,13},{... | collective-permute-start | bytes 8257544 | tf_op jit(solution)/shard_map/ppermute | solution.py:171
  386.4 19.2 %copy-start.7 = (bf16[512,1344]{0,1:T(8,128)(2,1)}, bf16[512,1344]{0,1:T(8,128)(2,1)S(1)}, u32[]{:S(2)}) copy-start(bf16[512,1344]{0,1:T(8,128)(2,1)S(1)} %collective-permute-done.8) | copy-start | bytes 4128772
  386.4 179.0 %collective-permute-start.13 = (bf16[2048,672]{0,1:T(8,128)(2,1)}, bf16[2048,672]{0,1:T(8,128)(2,1)}, u32[]{:S(2)}, u32[]{:S(2)}) collective-permute-start(bf16[2048,672]{0,1:T(8,128)(2,1)} %get-tuple-element.16), channel_id=1, source_target_pairs={{0,16},{4,20},{8,24},{12,28},{16,0},{20,4},{24,8},{28,12},{1,17},{... | collective-permute-start | bytes 8257544 | tf_op jit(solution)/shard_map/ppermute | solution.py:171
  386.5 19.2 %copy-start.9 = (bf16[512,1344]{0,1:T(8,128)(2,1)}, bf16[512,1344]{0,1:T(8,128)(2,1)S(1)}, u32[]{:S(2)}) copy-start(bf16[512,1344]{0,1:T(8,128)(2,1)S(1)} %collective-permute-done.7) | copy-start | bytes 4128772
  386.5 209.2 %collective-permute-start.12 = (bf16[2048,672]{0,1:T(8,128)(2,1)}, bf16[2048,672]{0,1:T(8,128)(2,1)}, u32[]{:S(2)}, u32[]{:S(2)}) collective-permute-start(bf16[2048,672]{0,1:T(8,128)(2,1)} %get-tuple-element.17), channel_id=1, source_target_pairs={{0,20},{4,24},{8,28},{12,0},{16,4},{20,8},{24,12},{28,16},{1,21},{... | collective-permute-start | bytes 8257544 | tf_op jit(solution)/shard_map/ppermute | solution.py:171
  387.4 208.2 %collective-permute-start.11 = (bf16[2048,672]{0,1:T(8,128)(2,1)}, bf16[2048,672]{0,1:T(8,128)(2,1)}, u32[]{:S(2)}, u32[]{:S(2)}) collective-permute-start(bf16[2048,672]{0,1:T(8,128)(2,1)} %get-tuple-element.18), channel_id=1, source_target_pairs={{0,24},{4,28},{8,0},{12,4},{16,8},{20,12},{24,16},{28,20},{1,25},{... | collective-permute-start | bytes 8257544 | tf_op jit(solution)/shard_map/ppermute | solution.py:171
  405.6 190.0 %collective-permute-start.10 = (bf16[2048,672]{0,1:T(8,128)(2,1)}, bf16[2048,672]{0,1:T(8,128)(2,1)}, u32[]{:S(2)}, u32[]{:S(2)}) collective-permute-start(bf16[2048,672]{0,1:T(8,128)(2,1)} %get-tuple-element.12), channel_id=1, source_target_pairs={{0,28},{4,0},{8,4},{12,8},{16,12},{20,16},{24,20},{28,24},{1,29},{... | collective-permute-start | bytes 8257544 | tf_op jit(solution)/shard_map/ppermute | solution.py:171
  409.3 2.4 copy-start.8
  409.3 2.4 copy-start.10
